TPU v7x, 512 devices: a whole 4x8x8 slice. The times are simulated.
512 devices in a mesh: dp: 8 (over z), expert: 16 (over y, core), etp: 4 (over x).
Axes of the slice: x: 4, y: 8, z: 8, core: 2. Of those that a mesh axis runs over, the one named last changes fastest.
Arguments:
- tokens: bfloat16 [3072, 4096], P(('dp', 'expert')), may hold values from -6 to 6
- cotangent: bfloat16 [3072, 4096], P(('dp', 'expert')), may hold values from -3 to 3
- route_weights: float32 [3072, 8], P(('dp', 'expert')), may hold values from 0.05 to 0.3
- expert_ids: int32 [3072, 8], P(('dp', 'expert')), may hold values from 0 to 15, as said below
- w_gate: bfloat16 [16, 1536, 4096], P('expert', 'etp', 'dp'), may hold values from -0.09375 to 0.09375
- w_up: bfloat16 [16, 1536, 4096], P('expert', 'etp', 'dp'), may hold values from -0.09375 to 0.09375
- w_down: bfloat16 [16, 1536, 4096], P('expert', 'etp', 'dp'), may hold values from -0.15625 to 0.15625
Outputs:
- mixed: bfloat16 [3072, 4096], P(('dp', 'expert'), 'etp')
- grad_tokens: bfloat16 [3072, 4096], P(('dp', 'expert'), 'etp')
- grad_gate: float32 [16, 1536, 4096], P('expert', 'etp', 'dp')
Inputs may be any that keep to these rules, and one draw needn't show every extreme that they name: `expert_ids`: each row names 8 different experts. Within each aligned block of 24 rows no expert is named by more than 16 rows; in every run of 16 consecutive blocks starting at a multiple of 16, one expert is named by exactly 16 rows of every block.
All inputs are finite; a program needn't handle non-finite values.
Results may differ from a plain program's by a relative error of at most 0.012.
Values may be sent and summed in bfloat16 or wider, within the bound.
No kernel may reach another device: no remote copies, remote signals or barrier semaphores. Data moves between devices by JAX's collectives and lax.ppermute only.
A program may use at most 64 MiB of HBM per device.

v0:
```python
import jax
import jax.numpy as jnp
from jax import lax
from jax.sharding import PartitionSpec as P


def on_device(tokens, cotangent, route_weights, expert_ids, w_gate, w_up, w_down):
    tok_count, model_width = tokens.shape
    top_count = expert_ids.shape[1]
    experts = lax.axis_size("expert")
    capacity = tok_count // experts * top_count + min(top_count, tok_count % experts)
    slot_rows = experts * capacity
    named_count = jnp.sum(
        (expert_ids[:, :, None] == jnp.arange(experts, dtype=jnp.int32)).astype(jnp.int32), axis=1
    )
    before = jnp.cumsum(named_count, axis=0) - named_count
    position = jnp.take_along_axis(before, expert_ids, axis=1)
    slot_index = (expert_ids * capacity + position).reshape(-1)
    copies = jnp.broadcast_to(tokens[:, None, :], (tok_count, top_count, model_width)).reshape(
        -1, model_width
    )
    scaled = (
        (route_weights[:, :, None] * cotangent[:, None, :].astype(jnp.float32))
        .astype(jnp.bfloat16)
        .reshape(-1, model_width)
    )
    empty_slots = jnp.zeros((slot_rows, model_width), jnp.bfloat16)
    send_rows = empty_slots.at[slot_index].set(copies).reshape(experts, capacity, model_width)
    send_grads = empty_slots.at[slot_index].set(scaled).reshape(experts, capacity, model_width)
    recv_rows, recv_grads = (
        lax.all_to_all(send_rows, "expert", split_axis=0, concat_axis=0, tiled=True),
        lax.all_to_all(send_grads, "expert", split_axis=0, concat_axis=0, tiled=True),
    )
    flat_rows = recv_rows.reshape(slot_rows, model_width)
    flat_grads = recv_grads.reshape(slot_rows, model_width)
    gate_full, up_full, down_full = (
        lax.all_gather(w_gate[0], "dp", axis=1, tiled=True),
        lax.all_gather(w_up[0], "dp", axis=1, tiled=True),
        lax.all_gather(w_down[0], "dp", axis=1, tiled=True),
    )
    contract_last = (((1,), (1,)), ((), ()))
    gate_value = lax.dot_general(
        flat_rows, gate_full, contract_last, preferred_element_type=jnp.float32
    )
    up_value = lax.dot_general(
        flat_rows, up_full, contract_last, preferred_element_type=jnp.float32
    )
    sigmoid_gate = jax.nn.sigmoid(gate_value)
    active = gate_value * sigmoid_gate
    hidden = (active * up_value).astype(jnp.bfloat16)
    mixed_slots = jnp.dot(hidden, down_full, preferred_element_type=jnp.float32).astype(
        jnp.bfloat16
    )
    d_hidden = lax.dot_general(
        flat_grads, down_full, contract_last, preferred_element_type=jnp.float32
    )
    d_gate = (
        d_hidden * up_value * sigmoid_gate * (1.0 + gate_value * (1.0 - sigmoid_gate))
    ).astype(jnp.bfloat16)
    d_up = (d_hidden * active).astype(jnp.bfloat16)
    input_slots = (
        jnp.dot(d_gate, gate_full, preferred_element_type=jnp.float32)
        + jnp.dot(d_up, up_full, preferred_element_type=jnp.float32)
    ).astype(jnp.bfloat16)
    weight_grads = lax.psum_scatter(
        lax.dot_general(
            flat_rows, d_gate, (((0,), (0,)), ((), ())), preferred_element_type=jnp.float32
        ).astype(jnp.bfloat16),
        "dp",
        scatter_dimension=0,
        tiled=True,
    ).astype(jnp.float32)
    grad_gate = jnp.transpose(weight_grads)[None]
    back_mixed, back_input = (
        lax.all_to_all(
            mixed_slots.reshape(experts, capacity, model_width),
            "expert",
            split_axis=0,
            concat_axis=0,
            tiled=True,
        ),
        lax.all_to_all(
            input_slots.reshape(experts, capacity, model_width),
            "expert",
            split_axis=0,
            concat_axis=0,
            tiled=True,
        ),
    )
    token_mixed = back_mixed.reshape(slot_rows, model_width)[slot_index].reshape(
        tok_count, top_count, model_width
    )
    token_input = back_input.reshape(slot_rows, model_width)[slot_index].reshape(
        tok_count, top_count, model_width
    )
    mixed_part = jnp.sum(route_weights[:, :, None] * token_mixed.astype(jnp.float32), axis=1)
    input_part = jnp.sum(token_input.astype(jnp.float32), axis=1)
    mixed, grad_tokens = (
        lax.psum_scatter(
            mixed_part.astype(jnp.bfloat16), "etp", scatter_dimension=1, tiled=True
        ).astype(jnp.float32),
        lax.psum_scatter(
            input_part.astype(jnp.bfloat16), "etp", scatter_dimension=1, tiled=True
        ).astype(jnp.float32),
    )
    return (mixed.astype(jnp.bfloat16), grad_tokens.astype(jnp.bfloat16), grad_gate)


def solution(mesh):
    in_specs = (
        P(("dp", "expert"), None),
        P(("dp", "expert"), None),
        P(("dp", "expert"), None),
        P(("dp", "expert"), None),
        P("expert", "etp", "dp"),
        P("expert", "etp", "dp"),
        P("expert", "etp", "dp"),
    )
    out_specs = (P(("dp", "expert"), "etp"), P(("dp", "expert"), "etp"), P("expert", "etp", "dp"))
    return jax.shard_map(
        on_device, mesh=mesh, in_specs=in_specs, out_specs=out_specs, check_vma=False
    )
```

profile of v0, /device:TPU:8, one launch (start us, length us, event | category | flops | bytes accessed | tf_op | source)
XLA Modules:
  0.0 312.0 jit_solution(12427213311101825373)
XLA Ops:
  7.2 0.0 all-gather.9.cloned.1.call-start
  7.2 0.7 all-gather.9.cloned.1.call-update
  7.9 0.0 all-gather.11.cloned.1.call-start
  8.0 0.7 all-gather.11.cloned.1.call-update
  8.7 0.8 copy.22
  9.4 0.7 convert_reduce_fusion
  10.1 0.1 copy.26
  10.3 0.1 reshape.117
  10.4 1.6 gather_fusion.2
  12.0 0.1 reshape.120
  12.1 0.1 reshape.88
  12.2 4.4 %scatter_custom_fusion = bf16[256,4096]{1,0:T(8,128)(2,1)} fusion(s32[192]{0:T(256)S(1)} %bitcast.61, bf16[]{:T(256)} %constant.10.clone.1, bf16[24,4096]{1,0:T(8,128)(2,1)S(1)} %copy-done), kind=kCustom, calls=%fused_computation.25 | custom fusion | bytes 2293762 | tf_op jit(solution)/shard_map/scatter | solution.py:28
  16.6 9.5 %all-to-all-start = ((bf16[16,16,4096]{2,1,0:T(8,128)(2,1)}), bf16[16,16,4096]{2,1,0:T(8,128)(2,1)S(1)}, u32[]{:S(2)}, u32[]{:S(2)}) async-start(bf16[16,16,4096]{2,1,0:T(8,128)(2,1)} %bitcast.59), calls=%async_computation | async-start | bytes 4194304 | tf_op jit(solution)/shard_map/all_to_all | solution.py:31
  26.0 0.0 all-gather.7.cloned.1.call-start
  26.1 0.7 all-gather.7.cloned.1.call-update
  26.8 0.1 copy.21
  26.9 0.1 mul.59
  27.0 4.3 %scatter_custom_fusion.1 = bf16[256,4096]{1,0:T(8,128)(2,1)} fusion(s32[192]{0:T(256)S(1)} %bitcast.62, f32[24,4096]{1,0:T(8,128)S(1)} %convert_element_type.51, f32[192]{0:T(256)S(1)} %mul.59, bf16[]{:T(256)} %constant.10.clone.1), kind=kCustom, calls=%fused_computation.23 | custom fusion | flops 1572864 | bytes 2491394 | tf_op jit(solution)/shard_map/scatter | solution.py:29
  31.3 42.1 %all-to-all-done = bf16[16,16,4096]{2,1,0:T(8,128)(2,1)S(1)} async-done(((bf16[16,16,4096]{2,1,0:T(8,128)(2,1)}), bf16[16,16,4096]{2,1,0:T(8,128)(2,1)S(1)}, u32[]{:S(2)}, u32[]{:S(2)}) %all-to-all-start) | async-done | bytes 2097184 | tf_op jit(solution)/shard_map/all_to_all | solution.py:31
  73.4 6.6 %all-to-all-start.2 = ((bf16[16,16,4096]{2,1,0:T(8,128)(2,1)}), bf16[16,16,4096]{2,1,0:T(8,128)(2,1)}, u32[]{:S(2)}, u32[]{:S(2)}) async-start(bf16[16,16,4096]{2,1,0:T(8,128)(2,1)} %bitcast.60), calls=%async_computation.3 | async-start | bytes 4194304 | tf_op jit(solution)/shard_map/all_to_all | solution.py:32
  80.0 0.0 all-gather.9.cloned.1.call-done
  80.0 3.9 %fusion.7 = f32[256,384]{1,0:T(8,128)} fusion(bf16[256,4096]{1,0:T(8,128)(2,1)S(1)} %bitcast.54, bf16[1,384,4096]{2,1,0:T(8,128)(2,1)} %all-gather.9.cloned.1.call-done), kind=kOutput, calls=%fused_computation.17 | convolution fusion | flops 805306368 | bytes 5636096 | tf_op jit(solution)/shard_map/dot_general | solution.py:45
  83.9 43.6 %all-to-all-done.2 = bf16[16,16,4096]{2,1,0:T(8,128)(2,1)} async-done(((bf16[16,16,4096]{2,1,0:T(8,128)(2,1)}), bf16[16,16,4096]{2,1,0:T(8,128)(2,1)}, u32[]{:S(2)}, u32[]{:S(2)}) %all-to-all-start.2) | async-done | bytes 2097184 | tf_op jit(solution)/shard_map/all_to_all | solution.py:32
  127.5 3.8 %fusion.3 = f32[256,384]{1,0:T(8,128)S(1)} fusion(bf16[256,4096]{1,0:T(8,128)(2,1)} %bitcast.13, bf16[1,384,4096]{2,1,0:T(8,128)(2,1)} %all-gather.11.cloned.1.call-done), kind=kOutput, calls=%fused_computation.13 | convolution fusion | flops 805306368 | bytes 5636096 | tf_op jit(solution)/shard_map/dot_general | solution.py:54
  131.3 29.1 %all-gather.7.cloned.1.call-done = bf16[1,384,4096]{2,1,0:T(8,128)(2,1)} async-done(((bf16[1,384,512]{2,1,0:T(8,128)(2,1)}), bf16[1,384,4096]{2,1,0:T(8,128)(2,1)}) %all-gather.7.cloned.1.call-update) | async-done | bytes 3145744 | tf_op jit(solution)/shard_map/all_gather | solution.py:37
  160.4 3.4 %multiply_convert_fusion.1 = (bf16[256,384]{1,0:T(8,128)(2,1)S(1)}, f32[256,384]{1,0:T(8,128)S(1)}) fusion(f32[256,384]{1,0:T(8,128)S(1)} %fusion.3, f32[256,384]{1,0:T(8,128)} %fusion.7, bf16[256,4096]{1,0:T(8,128)(2,1)S(1)} %bitcast.55, bf16[1,384,4096]{2,1,0:T(8,128)(2,1)} %all-gather.7.cloned.1.call-done), kind=kOutput, calls=%fused_computation.34 | convolution fusion | flops 806289408 | bytes 6619136 | tf_op jit(solution)/shard_map/dot_general | solution.py:42
  163.8 2.6 convolution_convert_fusion.1
  166.4 7.3 %all-to-all-start.1 = ((bf16[16,16,4096]{2,1,0:T(8,128)(2,1)}), bf16[16,16,4096]{2,1,0:T(8,128)(2,1)S(1)}, u32[]{:S(2)}, u32[]{:S(2)}) async-start(bf16[16,16,4096]{2,1,0:T(8,128)(2,1)} %bitcast.58), calls=%async_computation.1 | async-start | bytes 4194304 | tf_op jit(solution)/shard_map/all_to_all | solution.py:75
  173.7 0.0 reduce-scatter.8.cloned.1.call-start
  173.8 4.6 %convolution_convert_fusion = bf16[4096,384]{1,0:T(8,128)(2,1)} fusion(bf16[256,4096]{1,0:T(8,128)(2,1)} %bitcast.56, bf16[256,384]{1,0:T(8,128)(2,1)S(1)} %get-tuple-element.12), kind=kOutput, calls=%fused_computation.5 | convolution fusion | flops 806879232 | bytes 5439488 | tf_op jit(solution)/shard_map/dot_general | solution.py:66
  178.3 0.0 reduce-scatter.8.cloned.1.call-update
  178.4 3.3 %fusion.9 = f32[256,4096]{1,0:T(8,128)S(1)} fusion(bf16[256,384]{1,0:T(8,128)(2,1)S(1)} %get-tuple-element.12, bf16[1,384,4096]{2,1,0:T(8,128)(2,1)} %all-gather.7.cloned.1.call-done), kind=kOutput, calls=%fused_computation.19 | convolution fusion | flops 805306368 | bytes 7536640 | tf_op jit(solution)/shard_map/dot_general | solution.py:62
  181.7 2.7 fusion
  184.3 36.8 %all-to-all-done.1 = bf16[16,16,4096]{2,1,0:T(8,128)(2,1)S(1)} async-done(((bf16[16,16,4096]{2,1,0:T(8,128)(2,1)}), bf16[16,16,4096]{2,1,0:T(8,128)(2,1)S(1)}, u32[]{:S(2)}, u32[]{:S(2)}) %all-to-all-start.1) | async-done | bytes 2097184 | tf_op jit(solution)/shard_map/all_to_all | solution.py:75
  221.1 6.5 %all-to-all-start.3 = ((bf16[16,16,4096]{2,1,0:T(8,128)(2,1)}), bf16[16,16,4096]{2,1,0:T(8,128)(2,1)}, u32[]{:S(2)}, u32[]{:S(2)}) async-start(bf16[16,16,4096]{2,1,0:T(8,128)(2,1)} %bitcast.57), calls=%async_computation.4 | async-start | bytes 4194304 | tf_op jit(solution)/shard_map/all_to_all | solution.py:82
  227.7 0.0 reduce-scatter.4.cloned.1.call-start
  227.7 2.7 gather_fusion
  230.4 3.3 %fusion.1 = bf16[24,4096]{1,0:T(8,128)(2,1)} fusion(bf16[192,4096]{1,0:T(8,128)(2,1)} %gather_fusion, f32[24,8]{1,0:T(8,128)S(1)} %copy.21), kind=kLoop, calls=%fused_computation.10 | loop fusion | flops 2260992 | bytes 1770240 | tf_op jit(solution)/shard_map/reduce_sum | solution.py:96
  233.7 0.0 reduce-scatter.4.cloned.1.call-update
  233.8 0.0 reduce-scatter.6.cloned.1.call-start
  233.8 41.3 %all-to-all-done.3 = bf16[16,16,4096]{2,1,0:T(8,128)(2,1)} async-done(((bf16[16,16,4096]{2,1,0:T(8,128)(2,1)}), bf16[16,16,4096]{2,1,0:T(8,128)(2,1)}, u32[]{:S(2)}, u32[]{:S(2)}) %all-to-all-start.3) | async-done | bytes 2097184 | tf_op jit(solution)/shard_map/all_to_all | solution.py:82
  275.1 4.9 %gather_fusion.1 = bf16[192,4096]{1,0:T(8,128)(2,1)S(1)} fusion(bf16[256,4096]{1,0:T(8,128)(2,1)} %bitcast.15, s32[1024]{0:T(1024)S(1)} %pad_clamp_fusion), kind=kCustom, calls=%fused_computation.1 | custom fusion | bytes 3146496 | tf_op jit(solution)/shard_map/gather | solution.py:93
  280.1 1.7 bitcast_reduce_fusion
  281.8 0.0 reduce-scatter.6.cloned.1.call-update
  281.8 0.0 reduce-scatter.8.cloned.1.call-done
  281.8 1.0 convert_bitcast_fusion
  282.9 1.1 copy.29
  284.0 21.1 %reduce-scatter.6.cloned.1.call-done = bf16[24,1024]{1,0:T(8,128)(2,1)} async-done(((bf16[24,4096]{1,0:T(8,128)(2,1)}), bf16[24,1024]{1,0:T(8,128)(2,1)}) %reduce-scatter.6.cloned.1.call-update) | async-done | bytes 49168 | tf_op jit(solution)/shard_map/reduce_scatter | solution.py:102
  (23 shorter events, 0.1 us)
Async XLA Ops:
  7.2 5.0 %copy-start = (bf16[24,4096]{1,0:T(8,128)(2,1)S(1)}, bf16[24,4096]{1,0:T(8,128)(2,1)}, u32[]{:S(2)}) copy-start(bf16[24,4096]{1,0:T(8,128)(2,1)} %param.7) | copy-start | bytes 589828
  7.2 72.8 %all-gather.9.cloned.1.call-start = ((), (), s32[]{:S(2)}) async-start(), calls=%async_computation.11 | async-start | bytes 3538944 | tf_op jit(solution)/shard_map/all_gather | solution.py:38
  7.9 119.6 %all-gather.11.cloned.1.call-start = ((), (), s32[]{:S(2)}) async-start(), calls=%async_computation.12 | async-start | bytes 3538944 | tf_op jit(solution)/shard_map/all_gather | solution.py:39
  16.6 10.2 %copy-start.5 = (bf16[24,4096]{1,0:T(8,128)(2,1)S(1)}, bf16[24,4096]{1,0:T(8,128)(2,1)}, u32[]{:S(2)}) copy-start(bf16[24,4096]{1,0:T(8,128)(2,1)} %param.8) | copy-start | bytes 589828
  16.6 10.3 %copy-start.6 = (f32[24,8]{0,1:T(8,128)S(1)}, f32[24,8]{0,1:T(8,128)}, u32[]{:S(2)}) copy-start(f32[24,8]{0,1:T(8,128)} %param.9) | copy-start | bytes 2308
  16.6 56.9 %all-to-all-start = ((bf16[16,16,4096]{2,1,0:T(8,128)(2,1)}), bf16[16,16,4096]{2,1,0:T(8,128)(2,1)S(1)}, u32[]{:S(2)}, u32[]{:S(2)}) async-start(bf16[16,16,4096]{2,1,0:T(8,128)(2,1)} %bitcast.59), calls=%async_computation | async-start | bytes 4194304 | tf_op jit(solution)/shard_map/all_to_all | solution.py:31
  26.0 134.3 %all-gather.7.cloned.1.call-start = ((), (), s32[]{:S(2)}) async-start(), calls=%async_computation.10 | async-start | bytes 3538944 | tf_op jit(solution)/shard_map/all_gather | solution.py:37
  73.4 86.9 %copy-start.1 = (bf16[16,16,4096]{2,1,0:T(8,128)(2,1)}, bf16[16,16,4096]{2,1,0:T(8,128)(2,1)S(1)}, u32[]{:S(2)}) copy-start(bf16[16,16,4096]{2,1,0:T(8,128)(2,1)S(1)} %all-to-all-done) | copy-start | bytes 6291460
  73.4 54.1 %all-to-all-start.2 = ((bf16[16,16,4096]{2,1,0:T(8,128)(2,1)}), bf16[16,16,4096]{2,1,0:T(8,128)(2,1)}, u32[]{:S(2)}, u32[]{:S(2)}) async-start(bf16[16,16,4096]{2,1,0:T(8,128)(2,1)} %bitcast.60), calls=%async_computation.3 | async-start | bytes 4194304 | tf_op jit(solution)/shard_map/all_to_all | solution.py:32
  160.4 3.4 %copy-start.2 = (bf16[1,384,4096]{2,1,0:T(8,128)(2,1)S(1)}, bf16[1,384,4096]{2,1,0:T(8,128)(2,1)}, u32[]{:S(2)}) copy-start(bf16[1,384,4096]{2,1,0:T(8,128)(2,1)} %all-gather.11.cloned.1.call-done) | copy-start | bytes 9437188
  160.4 3.5 %copy-start.4 = (f32[256,384]{1,0:T(8,128)S(1)}, f32[256,384]{1,0:T(8,128)}, u32[]{:S(2)}) copy-start(f32[256,384]{1,0:T(8,128)} %fusion.7) | copy-start | bytes 1179652
  166.4 54.7 %all-to-all-start.1 = ((bf16[16,16,4096]{2,1,0:T(8,128)(2,1)}), bf16[16,16,4096]{2,1,0:T(8,128)(2,1)S(1)}, u32[]{:S(2)}, u32[]{:S(2)}) async-start(bf16[16,16,4096]{2,1,0:T(8,128)(2,1)} %bitcast.58), calls=%async_computation.1 | async-start | bytes 4194304 | tf_op jit(solution)/shard_map/all_to_all | solution.py:75
  173.7 108.1 %reduce-scatter.8.cloned.1.call-start = ((), (), s32[]{:S(2)}) async-start(), calls=%async_computation.9 | async-start | bytes 3538944 | tf_op jit(solution)/shard_map/reduce_scatter | solution.py:65
  178.4 3.3 %copy-start.3 = (bf16[1,384,4096]{2,1,0:T(8,128)(2,1)S(1)}, bf16[1,384,4096]{2,1,0:T(8,128)(2,1)}, u32[]{:S(2)}) copy-start(bf16[1,384,4096]{2,1,0:T(8,128)(2,1)} %all-gather.9.cloned.1.call-done) | copy-start | bytes 9437188
  221.1 54.0 %all-to-all-start.3 = ((bf16[16,16,4096]{2,1,0:T(8,128)(2,1)}), bf16[16,16,4096]{2,1,0:T(8,128)(2,1)}, u32[]{:S(2)}, u32[]{:S(2)}) async-start(bf16[16,16,4096]{2,1,0:T(8,128)(2,1)} %bitcast.57), calls=%async_computation.4 | async-start | bytes 4194304 | tf_op jit(solution)/shard_map/all_to_all | solution.py:82
  227.7 56.4 %reduce-scatter.4.cloned.1.call-start = ((), (), s32[]{:S(2)}) async-start(), calls=%async_computation.7 | async-start | bytes 245760 | tf_op jit(solution)/shard_map/reduce_scatter | solution.py:99
  233.8 71.4 %reduce-scatter.6.cloned.1.call-start = ((), (), s32[]{:S(2)}) async-start(), calls=%async_computation.8 | async-start | bytes 245760 | tf_op jit(solution)/shard_map/reduce_scatter | solution.py:102
Sparse Core Ops, SparseCore 0:
  10.1 52.9 all-gather.8
  65.2 46.4 all-gather.10
  113.8 46.4 all-gather.6
  178.5 48.1 reduce-scatter.7
  233.9 23.8 reduce-scatter.3
  281.9 23.1 reduce-scatter.5
where the time goes:
time: 313 us; the launch traced here: 312 us
  waiting for transfers between devices  216 us (69%)
  starting transfers between devices  30.1 us (10%)
  matrix products  24.2 us (8%)
  local copies, waits for them, and re-layouts  16.1 us (5%)
  between operations  14.3 us (5%)
  other arithmetic  11.2 us (4%)
    all_to_all x1, waiting for transfers between devices, on_device(): lax.all_to_all(send_grads, 'expert', split_axis=0, concat_axis=0, tiled=T...  43.6 us
    all_to_all x1, waiting for transfers between devices, on_device(): lax.all_to_all(send_rows, 'expert', split_axis=0, concat_axis=0, tiled=True)  42.1 us
    all_to_all x1, waiting for transfers between devices, on_device(): lax.all_to_all(input_slots.reshape(experts, capacity, model_width), 'expe...  41.3 us
    all_to_all x1, waiting for transfers between devices, on_device(): lax.all_to_all(mixed_slots.reshape(experts, capacity, model_width), 'expe...  36.8 us
    all_gather x1, waiting for transfers between devices, on_device(): lax.all_gather(w_gate[0], 'dp', axis=1, tiled=True)  29.1 us
    reduce_scatter x1, waiting for transfers between devices, on_device(): lax.psum_scatter(input_part.astype(jnp.bfloat16), 'etp', scatter_dimensio...  21.1 us
    all_to_all x1, starting transfers between devices, on_device(): lax.all_to_all(send_rows, 'expert', split_axis=0, concat_axis=0, tiled=True)  9.47 us
    all_to_all x1, starting transfers between devices, on_device(): lax.all_to_all(mixed_slots.reshape(experts, capacity, model_width), 'expe...  7.29 us
  transfers between devices with their start and end apart: 10, of which 6 were waited for; matrix products, arithmetic and copies ran while one was open for 15% of the time, Pallas kernels for 0%

commit v1 on v0

--- a/solution.py
+++ b/solution.py
@@ -2,6 +2,12 @@
 import jax.numpy as jnp
 from jax import lax
 from jax.sharding import PartitionSpec as P
+
+
+def gather_by_exchange(x, axis, dim):
+    length = lax.axis_size(axis)
+    repeats = [length if d == dim else 1 for d in range(x.ndim)]
+    return lax.all_to_all(jnp.tile(x, repeats), axis, split_axis=dim, concat_axis=dim, tiled=True)
 
 
 def on_device(tokens, cotangent, route_weights, expert_ids, w_gate, w_up, w_down):
@@ -34,7 +40,7 @@
     flat_rows = recv_rows.reshape(slot_rows, model_width)
     flat_grads = recv_grads.reshape(slot_rows, model_width)
     gate_full, up_full, down_full = (
-        lax.all_gather(w_gate[0], "dp", axis=1, tiled=True),
+        gather_by_exchange(w_gate[0], "dp", 1),
         lax.all_gather(w_up[0], "dp", axis=1, tiled=True),
         lax.all_gather(w_down[0], "dp", axis=1, tiled=True),
     )

time: 313 us -> 389 us (1.24)
  waiting for transfers between devices: 216 us -> 280 us
  starting transfers between devices: 30.1 us -> 37.5 us
  local copies, waits for them, and re-layouts: 16.1 us -> 23.4 us
    all_to_all x0 -> x1, waiting for transfers between devices: none -> 95.7 us  [gather_by_exchange(): lax.all_to_all(jnp.tile(x, repeats), axis, split_axis=dim, concat_axis=di...]
    all_gather x1 -> x0, waiting for transfers between devices: 29.1 us -> none  [on_device(): lax.all_gather(w_gate[0], 'dp', axis=1, tiled=True)]
    all_to_all x0 -> x1, starting transfers between devices: none -> 8.66 us  [gather_by_exchange(): lax.all_to_all(jnp.tile(x, repeats), axis, split_axis=dim, concat_axis=di...]
    all_to_all x0 -> x1, local copies, waits for them, and re-layouts: none -> 4.76 us  [gather_by_exchange(): lax.all_to_all(jnp.tile(x, repeats), axis, split_axis=dim, concat_axis=di...]
    all_to_all x1, waiting for transfers between devices: 43.6 us -> 38.8 us  [on_device(): lax.all_to_all(send_grads, 'expert', split_axis=0, concat_axis=0, tiled=T...]
    all_to_all x1, waiting for transfers between devices: 42.1 us -> 46.7 us  [on_device(): lax.all_to_all(send_rows, 'expert', split_axis=0, concat_axis=0, tiled=True)]
  transfers between devices with their start and end apart: 10 -> 10, of which waited for: 6 -> 6; matrix products, arithmetic and copies ran while one was open for 15% -> 10% of each run, Pallas kernels for 0% -> 0%
where the time goes in v1:
time: 389 us; the launch traced here: 388 us
  waiting for transfers between devices  280 us (72%)
  starting transfers between devices  37.5 us (10%)
  local copies, waits for them, and re-layouts  23.4 us (6%)
  matrix products  22.4 us (6%)
  between operations  14 us (4%)
  other arithmetic  11.2 us (3%)
    all_to_all x1, waiting for transfers between devices, gather_by_exchange(): lax.all_to_all(jnp.tile(x, repeats), axis, split_axis=dim, concat_axis=di...  95.7 us
    all_to_all x1, waiting for transfers between devices, on_device(): lax.all_to_all(send_rows, 'expert', split_axis=0, concat_axis=0, tiled=True)  46.7 us
    all_to_all x1, waiting for transfers between devices, on_device(): lax.all_to_all(input_slots.reshape(experts, capacity, model_width), 'expe...  41.1 us
    all_to_all x1, waiting for transfers between devices, on_device(): lax.all_to_all(send_grads, 'expert', split_axis=0, concat_axis=0, tiled=T...  38.8 us
    all_to_all x1, waiting for transfers between devices, on_device(): lax.all_to_all(mixed_slots.reshape(experts, capacity, model_width), 'expe...  36.8 us
    reduce_scatter x1, waiting for transfers between devices, on_device(): lax.psum_scatter(input_part.astype(jnp.bfloat16), 'etp', scatter_dimensio...  19.4 us
    all_to_all x1, starting transfers between devices, on_device(): lax.all_to_all(send_rows, 'expert', split_axis=0, concat_axis=0, tiled=True)  9.47 us
    all_to_all x1, starting transfers between devices, gather_by_exchange(): lax.all_to_all(jnp.tile(x, repeats), axis, split_axis=dim, concat_axis=di...  8.66 us
  transfers between devices with their start and end apart: 10, of which 6 were waited for; matrix products, arithmetic and copies ran while one was open for 10% of the time, Pallas kernels for 0%

profile of v1, /device:TPU:8, one launch (start us, length us, event | category | flops | bytes accessed | tf_op | source)
XLA Modules:
  0.0 388.4 jit_solution(11934007203162887394)
XLA Ops:
  7.2 0.7 convert_reduce_fusion
  7.9 0.8 copy.39
  8.7 0.1 copy.43
  8.8 0.1 reshape.124
  8.9 1.6 gather_fusion.2
  10.5 0.1 reshape.127
  10.6 0.1 reshape.95
  10.7 4.3 %scatter_custom_fusion = bf16[256,4096]{1,0:T(8,128)(2,1)} fusion(s32[192]{0:T(256)S(1)} %bitcast.61, bf16[]{:T(256)} %constant.10.clone.1, bf16[24,4096]{1,0:T(8,128)(2,1)S(1)} %copy-done), kind=kCustom, calls=%fused_computation.21 | custom fusion | bytes 2293762 | tf_op jit(solution)/shard_map/scatter | solution.py:34
  15.0 9.5 %all-to-all-start = ((bf16[16,16,4096]{2,1,0:T(8,128)(2,1)}), bf16[16,16,4096]{2,1,0:T(8,128)(2,1)S(1)}, u32[]{:S(2)}, u32[]{:S(2)}) async-start(bf16[16,16,4096]{2,1,0:T(8,128)(2,1)} %bitcast.59), calls=%async_computation | async-start | bytes 4194304 | tf_op jit(solution)/shard_map/all_to_all | solution.py:37
  24.5 0.0 all-gather.5.cloned.1.call-start
  24.5 0.7 all-gather.5.cloned.1.call-update
  25.2 46.7 %all-to-all-done = bf16[16,16,4096]{2,1,0:T(8,128)(2,1)S(1)} async-done(((bf16[16,16,4096]{2,1,0:T(8,128)(2,1)}), bf16[16,16,4096]{2,1,0:T(8,128)(2,1)S(1)}, u32[]{:S(2)}, u32[]{:S(2)}) %all-to-all-start) | async-done | bytes 2097184 | tf_op jit(solution)/shard_map/all_to_all | solution.py:37
  71.9 2.2 tile.9
  74.1 8.7 %all-to-all-start.1 = ((bf16[384,8,512]{2,0,1:T(8,128)(2,1)}), bf16[384,8,512]{2,0,1:T(8,128)(2,1)}, u32[]{:S(2)}, u32[]{:S(2)}) async-start(bf16[384,8,512]{2,0,1:T(8,128)(2,1)} %tile.9), calls=%async_computation.1 | async-start | bytes 6291456 | tf_op jit(solution)/shard_map/all_to_all | solution.py:10
  82.7 0.0 all-gather.7.cloned.1.call-start
  82.8 0.7 all-gather.7.cloned.1.call-update
  83.5 0.1 copy.38
  83.6 0.1 mul.59
  83.7 4.3 %scatter_custom_fusion.1 = bf16[256,4096]{1,0:T(8,128)(2,1)} fusion(s32[192]{0:T(256)S(1)} %bitcast.62, f32[24,4096]{1,0:T(8,128)S(1)} %convert_element_type.51, f32[192]{0:T(256)S(1)} %mul.59, bf16[]{:T(256)} %constant.10.clone.1), kind=kCustom, calls=%fused_computation.19 | custom fusion | flops 1572864 | bytes 2491394 | tf_op jit(solution)/shard_map/scatter | solution.py:35
  88.0 95.7 %all-to-all-done.1 = bf16[384,8,512]{2,0,1:T(8,128)(2,1)} async-done(((bf16[384,8,512]{2,0,1:T(8,128)(2,1)}), bf16[384,8,512]{2,0,1:T(8,128)(2,1)}, u32[]{:S(2)}, u32[]{:S(2)}) %all-to-all-start.1) | async-done | bytes 3145760 | tf_op jit(solution)/shard_map/all_to_all | solution.py:10
  183.7 5.8 %all-to-all-start.3 = ((bf16[16,16,4096]{2,1,0:T(8,128)(2,1)}), bf16[16,16,4096]{2,1,0:T(8,128)(2,1)}, u32[]{:S(2)}, u32[]{:S(2)}) async-start(bf16[16,16,4096]{2,1,0:T(8,128)(2,1)} %bitcast.58), calls=%async_computation.4 | async-start | bytes 4194304 | tf_op jit(solution)/shard_map/all_to_all | solution.py:38
  189.6 4.8 %copy.45 = bf16[384,8,512]{0,2,1:T(8,128)(2,1)} copy(bf16[384,8,512]{2,0,1:T(8,128)(2,1)} %all-to-all-done.1) | data formatting | bytes 6291456 | tf_op jit(solution)/shard_map/all_to_all | solution.py:10
  194.3 3.9 %fusion.7 = f32[256,384]{1,0:T(8,128)} fusion(bf16[256,4096]{1,0:T(8,128)(2,1)S(1)} %bitcast.51, bf16[1,384,4096]{2,1,0:T(8,128)(2,1)} %all-gather.5.cloned.1.call-done), kind=kOutput, calls=%fused_computation.17 | convolution fusion | flops 805306368 | bytes 5636096 | tf_op jit(solution)/shard_map/dot_general | solution.py:51
  198.3 38.8 %all-to-all-done.3 = bf16[16,16,4096]{2,1,0:T(8,128)(2,1)} async-done(((bf16[16,16,4096]{2,1,0:T(8,128)(2,1)}), bf16[16,16,4096]{2,1,0:T(8,128)(2,1)}, u32[]{:S(2)}, u32[]{:S(2)}) %all-to-all-start.3) | async-done | bytes 2097184 | tf_op jit(solution)/shard_map/all_to_all | solution.py:38
  237.1 3.9 %fusion.3 = f32[256,384]{1,0:T(8,128)S(1)} fusion(bf16[256,4096]{1,0:T(8,128)(2,1)} %bitcast.14, bf16[1,384,4096]{2,1,0:T(8,128)(2,1)} %all-gather.7.cloned.1.call-done), kind=kOutput, calls=%fused_computation.13 | convolution fusion | flops 805306368 | bytes 5636096 | tf_op jit(solution)/shard_map/dot_general | solution.py:60
  241.1 1.4 multiply_convert_fusion.1
  242.5 0.5 copy-done.3
  242.9 2.6 convolution_convert_fusion.1
  245.5 6.6 %all-to-all-start.2 = ((bf16[16,16,4096]{2,1,0:T(8,128)(2,1)}), bf16[16,16,4096]{2,1,0:T(8,128)(2,1)S(1)}, u32[]{:S(2)}, u32[]{:S(2)}) async-start(bf16[16,16,4096]{2,1,0:T(8,128)(2,1)} %bitcast.57), calls=%async_computation.2 | async-start | bytes 4194304 | tf_op jit(solution)/shard_map/all_to_all | solution.py:81
  252.1 0.0 reduce-scatter.8.cloned.1.call-start
  252.1 4.6 %convolution_convert_fusion = bf16[4096,384]{1,0:T(8,128)(2,1)} fusion(bf16[256,4096]{1,0:T(8,128)(2,1)} %bitcast.53, bf16[256,384]{1,0:T(8,128)(2,1)S(1)} %get-tuple-element.18), kind=kOutput, calls=%fused_computation.5 | convolution fusion | flops 806879232 | bytes 5439488 | tf_op jit(solution)/shard_map/dot_general | solution.py:72
  256.7 0.0 reduce-scatter.8.cloned.1.call-update
  256.7 3.3 fusion.23
  260.1 2.7 fusion
  262.7 36.8 %all-to-all-done.2 = bf16[16,16,4096]{2,1,0:T(8,128)(2,1)S(1)} async-done(((bf16[16,16,4096]{2,1,0:T(8,128)(2,1)}), bf16[16,16,4096]{2,1,0:T(8,128)(2,1)S(1)}, u32[]{:S(2)}, u32[]{:S(2)}) %all-to-all-start.2) | async-done | bytes 2097184 | tf_op jit(solution)/shard_map/all_to_all | solution.py:81
  299.5 6.5 %all-to-all-start.4 = ((bf16[16,16,4096]{2,1,0:T(8,128)(2,1)}), bf16[16,16,4096]{2,1,0:T(8,128)(2,1)}, u32[]{:S(2)}, u32[]{:S(2)}) async-start(bf16[16,16,4096]{2,1,0:T(8,128)(2,1)} %bitcast.56), calls=%async_computation.5 | async-start | bytes 4194304 | tf_op jit(solution)/shard_map/all_to_all | solution.py:88
  306.0 0.0 reduce-scatter.4.cloned.1.call-start
  306.1 2.7 gather_fusion
  308.8 3.3 fusion.1
  312.1 0.0 reduce-scatter.4.cloned.1.call-update
  312.1 0.3 reduce-scatter.6.cloned.1.call-start
  312.4 41.1 %all-to-all-done.4 = bf16[16,16,4096]{2,1,0:T(8,128)(2,1)} async-done(((bf16[16,16,4096]{2,1,0:T(8,128)(2,1)}), bf16[16,16,4096]{2,1,0:T(8,128)(2,1)}, u32[]{:S(2)}, u32[]{:S(2)}) %all-to-all-start.4) | async-done | bytes 2097184 | tf_op jit(solution)/shard_map/all_to_all | solution.py:88
  353.5 4.9 %gather_fusion.1 = bf16[192,4096]{1,0:T(8,128)(2,1)S(1)} fusion(bf16[256,4096]{1,0:T(8,128)(2,1)} %bitcast.16, s32[1024]{0:T(1024)S(1)} %pad_clamp_fusion), kind=kCustom, calls=%fused_computation.1 | custom fusion | bytes 3146496 | tf_op jit(solution)/shard_map/gather | solution.py:99
  358.4 1.7 bitcast_reduce_fusion
  360.2 0.0 reduce-scatter.8.cloned.1.call-done
  360.2 1.0 convert_bitcast_fusion
  361.2 1.1 copy.47
  362.4 19.4 %reduce-scatter.6.cloned.1.call-done = bf16[24,1024]{1,0:T(8,128)(2,1)} async-done(((bf16[24,4096]{1,0:T(8,128)(2,1)}), bf16[24,1024]{1,0:T(8,128)(2,1)}) %reduce-scatter.6.cloned.1.call-update) | async-done | bytes 49168 | tf_op jit(solution)/shard_map/reduce_scatter | solution.py:108
  (28 shorter events, 0.2 us)
Async XLA Ops:
  7.2 3.6 copy-start
  15.0 56.9 %copy-start.5 = (bf16[1,384,512]{2,1,0:T(8,128)(2,1)S(1)}, bf16[1,384,512]{2,1,0:T(8,128)(2,1)}, u32[]{:S(2)}) copy-start(bf16[1,384,512]{2,1,0:T(8,128)(2,1)} %param.11) | copy-start | bytes 1179652
  15.0 56.9 %all-to-all-start = ((bf16[16,16,4096]{2,1,0:T(8,128)(2,1)}), bf16[16,16,4096]{2,1,0:T(8,128)(2,1)S(1)}, u32[]{:S(2)}, u32[]{:S(2)}) async-start(bf16[16,16,4096]{2,1,0:T(8,128)(2,1)} %bitcast.59), calls=%async_computation | async-start | bytes 4194304 | tf_op jit(solution)/shard_map/all_to_all | solution.py:37
  24.5 169.8 %all-gather.5.cloned.1.call-start = ((), (), s32[]{:S(2)}) async-start(), calls=%async_computation.11 | async-start | bytes 3538944 | tf_op jit(solution)/shard_map/all_gather | solution.py:44
  71.9 169.1 %copy-start.1 = (bf16[16,16,4096]{2,1,0:T(8,128)(2,1)}, bf16[16,16,4096]{2,1,0:T(8,128)(2,1)S(1)}, u32[]{:S(2)}) copy-start(bf16[16,16,4096]{2,1,0:T(8,128)(2,1)S(1)} %all-to-all-done) | copy-start | bytes 6291460
  74.1 9.4 %copy-start.7 = (bf16[24,4096]{1,0:T(8,128)(2,1)S(1)}, bf16[24,4096]{1,0:T(8,128)(2,1)}, u32[]{:S(2)}) copy-start(bf16[24,4096]{1,0:T(8,128)(2,1)} %param.8) | copy-start | bytes 589828
  74.1 9.5 %copy-start.8 = (f32[24,8]{0,1:T(8,128)S(1)}, f32[24,8]{0,1:T(8,128)}, u32[]{:S(2)}) copy-start(f32[24,8]{0,1:T(8,128)} %param.9) | copy-start | bytes 2308
  74.1 109.7 %all-to-all-start.1 = ((bf16[384,8,512]{2,0,1:T(8,128)(2,1)}), bf16[384,8,512]{2,0,1:T(8,128)(2,1)}, u32[]{:S(2)}, u32[]{:S(2)}) async-start(bf16[384,8,512]{2,0,1:T(8,128)(2,1)} %tile.9), calls=%async_computation.1 | async-start | bytes 6291456 | tf_op jit(solution)/shard_map/all_to_all | solution.py:10
  82.7 154.4 %all-gather.7.cloned.1.call-start = ((), (), s32[]{:S(2)}) async-start(), calls=%async_computation.12 | async-start | bytes 3538944 | tf_op jit(solution)/shard_map/all_gather | solution.py:45
  183.7 53.3 %all-to-all-start.3 = ((bf16[16,16,4096]{2,1,0:T(8,128)(2,1)}), bf16[16,16,4096]{2,1,0:T(8,128)(2,1)}, u32[]{:S(2)}, u32[]{:S(2)}) async-start(bf16[16,16,4096]{2,1,0:T(8,128)(2,1)} %bitcast.58), calls=%async_computation.4 | async-start | bytes 4194304 | tf_op jit(solution)/shard_map/all_to_all | solution.py:38
  237.1 4.0 %copy-start.2 = (bf16[384,8,512]{0,2,1:T(8,128)(2,1)S(1)}, bf16[384,8,512]{0,2,1:T(8,128)(2,1)}, u32[]{:S(2)}) copy-start(bf16[384,8,512]{0,2,1:T(8,128)(2,1)} %copy.45) | copy-start | bytes 9437188
  237.1 4.0 %copy-start.6 = (f32[256,384]{1,0:T(8,128)S(1)}, f32[256,384]{1,0:T(8,128)}, u32[]{:S(2)}) copy-start(f32[256,384]{1,0:T(8,128)} %fusion.7) | copy-start | bytes 1179652
  241.0 1.9 copy-start.3
  245.5 53.9 %all-to-all-start.2 = ((bf16[16,16,4096]{2,1,0:T(8,128)(2,1)}), bf16[16,16,4096]{2,1,0:T(8,128)(2,1)S(1)}, u32[]{:S(2)}, u32[]{:S(2)}) async-start(bf16[16,16,4096]{2,1,0:T(8,128)(2,1)} %bitcast.57), calls=%async_computation.2 | async-start | bytes 4194304 | tf_op jit(solution)/shard_map/all_to_all | solution.py:81
  252.1 108.1 %reduce-scatter.8.cloned.1.call-start = ((), (), s32[]{:S(2)}) async-start(), calls=%async_computation.10 | async-start | bytes 3538944 | tf_op jit(solution)/shard_map/reduce_scatter | solution.py:71
  256.7 3.3 copy-start.4
  299.5 54.0 %all-to-all-start.4 = ((bf16[16,16,4096]{2,1,0:T(8,128)(2,1)}), bf16[16,16,4096]{2,1,0:T(8,128)(2,1)}, u32[]{:S(2)}, u32[]{:S(2)}) async-start(bf16[16,16,4096]{2,1,0:T(8,128)(2,1)} %bitcast.56), calls=%async_computation.5 | async-start | bytes 4194304 | tf_op jit(solution)/shard_map/all_to_all | solution.py:88
  306.0 56.4 %reduce-scatter.4.cloned.1.call-start = ((), (), s32[]{:S(2)}) async-start(), calls=%async_computation.8 | async-start | bytes 245760 | tf_op jit(solution)/shard_map/reduce_scatter | solution.py:105
  312.1 69.7 %reduce-scatter.6.cloned.1.call-start = ((), (), s32[]{:S(2)}) async-start(), calls=%async_computation.9 | async-start | bytes 245760 | tf_op jit(solution)/shard_map/reduce_scatter | solution.py:108
Sparse Core Ops, SparseCore 0:
  27.4 50.8 all-gather.4
  85.6 99.3 all-gather.6
  256.8 46.5 reduce-scatter.7
  312.2 22.2 reduce-scatter.3
  360.3 21.4 reduce-scatter.5
